TPU v7x, 128 devices: a whole 4x4x4 slice. The times are simulated.
128 devices in a mesh: region: 64 (over z, y, x), chan: 2 (over core).
Axes of the slice: x: 4, y: 4, z: 4, core: 2. Of those that a mesh axis runs over, the one named last changes fastest.
Arguments:
- features: bfloat16 [384, 196608], P('chan', 'region'), may hold values from -6 to 6
- gain: float32 [384], P('chan'), may hold values from 0.1 to 1.9
- bias: float32 [384], P('chan'), may hold values from -3 to 3
- live: int32 [64], P('region'), may hold values from 1024 to 3072, as said below
- neighbors: int32 [27, 196608], P(None, 'region'), may hold values from -1 to 196607, as said below
- weights: bfloat16 [27, 384, 384], P(None, 'chan'), may hold values from -0.0625 to 0.0625
- grad_out: bfloat16 [384, 196608], P('chan', 'region'), may hold values from -0.059814453 to 0.059814453
Outputs:
- conv_out: bfloat16 [384, 196608], P('chan', 'region')
- kernel_grad: float32 [27, 384, 384], P(None, 'chan')
Inputs may be any that keep to these rules, and one draw needn't show every extreme that they name: One region has all 3072 slots counted live. `neighbors`: an entry [k, i] is -1 or the index of a live site at most 256 away from i; every entry of a site that is not live is -1.
All inputs are finite; a program needn't handle non-finite values.
Results may differ from a plain program's by a relative error of at most 0.0049.
Values may be sent and summed in bfloat16 or wider, within the bound.
No kernel may reach another device: no remote copies, remote signals or barrier semaphores. Data moves between devices by JAX's collectives and lax.ppermute only.
A program may use at most 128 MiB of HBM per device.

v0:
```python
import jax
import jax.numpy as jnp
import numpy as np
from jax import lax
from jax.sharding import Mesh
from jax.sharding import PartitionSpec as P

SUB = ("z", "y", "x")


def region_sum(x):
    for axis in reversed(SUB):
        x = lax.psum(x, axis)
    return x


def padded(x, width):
    count = lax.axis_size(SUB)
    length = x.shape[0]
    up = [(i, (i + 1) % count) for i in range(count - 1)]
    down = [(j, i) for i, j in up]
    last = lax.slice_in_dim(x, length - width, length, axis=0)
    first = lax.slice_in_dim(x, 0, width, axis=0)
    before = lax.ppermute(last, SUB, up)
    after = lax.ppermute(first, SUB, down)
    return jnp.concatenate([before, x, after], axis=0)


def per_device(features, gain, bias, live, neighbors, weights, grad_out):
    channels, columns = features.shape
    border = columns // 12
    region_idx = lax.axis_index(SUB)
    column = jnp.arange(columns, dtype=jnp.int32)
    live_limit = live[0] - border
    live_mask = ((column < live_limit) | (column >= columns - border)).astype(jnp.float32)
    values = features.astype(jnp.float32)
    masked = values * live_mask[None, :]
    live_rows = jnp.sum(live_mask)
    totals, live_total = region_sum((jnp.sum(masked, axis=1), live_rows))
    average = totals / live_total
    centered = (values - average[:, None]) * live_mask[None, :]
    variance = region_sum(jnp.sum(centered * centered, axis=1)) / live_total
    factor = gain * lax.rsqrt(variance + 1e-05)
    normed = (
        jnp.maximum((values - average[:, None]) * factor[:, None] + bias[:, None], 0.0)
        * live_mask[None, :]
    )
    site_rows = jnp.transpose(normed).astype(jnp.bfloat16)
    own_chans = lax.all_gather(site_rows, "chan", axis=1, tiled=True)
    gathered = padded(own_chans, border)
    anchor = region_idx * columns - border
    extent = columns + 2 * border

    def offset_step(running, operand):
        kernel, targets = operand
        position = jnp.where(targets < 0, extent, targets - anchor)
        picked = jnp.take(gathered, position, axis=0, mode="fill", fill_value=0)
        running = running + lax.dot_general(
            kernel, picked, (((1,), (1,)), ((), ())), preferred_element_type=jnp.float32
        )
        grad_piece = jnp.dot(grad_out, picked, preferred_element_type=jnp.float32)
        return (running, grad_piece)

    start = jnp.zeros((weights.shape[1], columns), jnp.float32)
    conv_sum, grad_parts = lax.scan(offset_step, start, (weights, neighbors))
    kernel_grad = region_sum(grad_parts)
    return (conv_sum.astype(jnp.bfloat16), kernel_grad)


def sub_mesh(mesh):
    devices = np.asarray(mesh.devices)
    count = devices.shape[0]
    first = devices[:, 0]
    try:
        sizes = [len({d.coords[a] for d in first}) for a in (2, 1, 0)]
    except (AttributeError, IndexError, TypeError):
        sizes = [count, 1, 1]
    if int(np.prod(sizes)) != count:
        sizes = [count, 1, 1]
    return Mesh(devices.reshape(*sizes, devices.shape[1]), SUB + ("chan",))


def solution(mesh):
    sites = ("chan", SUB)
    return jax.shard_map(
        per_device,
        mesh=sub_mesh(mesh),
        in_specs=(
            P(*sites),
            P("chan"),
            P("chan"),
            P(SUB),
            P(None, SUB),
            P(None, "chan", None),
            P(*sites),
        ),
        out_specs=(P(*sites), P(None, "chan", None)),
        check_vma=False,
    )
```

profile of v0, /device:TPU:1, one launch (start us, length us, event | category | flops | bytes accessed | tf_op | source)
XLA Modules:
  0.0 1149.2 jit_solution(16765144622355839185)
XLA Ops:
  63.2 23.1 %all-gather.2.cloned.1.call-done = bf16[3072,384]{0,1:T(8,128)(2,1)} async-done(((bf16[3072,192]{0,1:T(8,128)(2,1)}), bf16[3072,384]{0,1:T(8,128)(2,1)}) %all-gather.2.cloned.1.call-update) | async-done | bytes 2359312 | tf_op jit(solution)/shard_map/all_gather | solution.py:49
  105.2 559.5 %while.13 = (s32[]{:T(128)}, f32[192,3072]{1,0:T(8,128)}, f32[27,192,384]{2,1,0:T(8,128)}, bf16[27,192,384]{2,1,0:T(8,128)(2,1)}, s32[27,3072]{1,0:T(8,128)}, /*...) while((s32[]{:T(128)}, f32[192,3072]{1,0:T(8,128)}, ...), condition=%wide.region_13.14_spmd.clone, body=%wide.region_12.13_spmd.clone.sunk | while | flops 909548544 | bytes 30030000 | solution.py:65
  106.2 13.0 %gather_fusion = bf16[3072,384]{1,0:T(8,128)(2,1)} fusion(bf16[3584,384]{1,0:T(8,128)(2,1)S(1)} %get-tuple-element.187, s32[3072]{0:T(1024)S(1)} %broadcast_clamp_fusion.2), kind=kCustom, calls=%fused_computation.clone.clone.1 | custom fusion | bytes 4730880 | tf_op jit(solution)/shard_map/while/body/eval_jaxpr/jit(_take)/gather | solution.py:57
  147.0 13.0 %gather_fusion = bf16[3072,384]{1,0:T(8,128)(2,1)} fusion(bf16[3584,384]{1,0:T(8,128)(2,1)S(1)} %get-tuple-element.187, s32[3072]{0:T(1024)S(1)} %broadcast_clamp_fusion.2), kind=kCustom, calls=%fused_computation.clone.clone.1 | custom fusion | bytes 4730880 | tf_op jit(solution)/shard_map/while/body/eval_jaxpr/jit(_take)/gather | solution.py:57
  167.7 13.0 %gather_fusion = bf16[3072,384]{1,0:T(8,128)(2,1)} fusion(bf16[3584,384]{1,0:T(8,128)(2,1)S(1)} %get-tuple-element.187, s32[3072]{0:T(1024)S(1)} %broadcast_clamp_fusion.2), kind=kCustom, calls=%fused_computation.clone.clone.1 | custom fusion | bytes 4730880 | tf_op jit(solution)/shard_map/while/body/eval_jaxpr/jit(_take)/gather | solution.py:57
  188.5 13.0 %gather_fusion = bf16[3072,384]{1,0:T(8,128)(2,1)} fusion(bf16[3584,384]{1,0:T(8,128)(2,1)S(1)} %get-tuple-element.187, s32[3072]{0:T(1024)S(1)} %broadcast_clamp_fusion.2), kind=kCustom, calls=%fused_computation.clone.clone.1 | custom fusion | bytes 4730880 | tf_op jit(solution)/shard_map/while/body/eval_jaxpr/jit(_take)/gather | solution.py:57
  209.2 13.0 %gather_fusion = bf16[3072,384]{1,0:T(8,128)(2,1)} fusion(bf16[3584,384]{1,0:T(8,128)(2,1)S(1)} %get-tuple-element.187, s32[3072]{0:T(1024)S(1)} %broadcast_clamp_fusion.2), kind=kCustom, calls=%fused_computation.clone.clone.1 | custom fusion | bytes 4730880 | tf_op jit(solution)/shard_map/while/body/eval_jaxpr/jit(_take)/gather | solution.py:57
  230.0 13.0 %gather_fusion = bf16[3072,384]{1,0:T(8,128)(2,1)} fusion(bf16[3584,384]{1,0:T(8,128)(2,1)S(1)} %get-tuple-element.187, s32[3072]{0:T(1024)S(1)} %broadcast_clamp_fusion.2), kind=kCustom, calls=%fused_computation.clone.clone.1 | custom fusion | bytes 4730880 | tf_op jit(solution)/shard_map/while/body/eval_jaxpr/jit(_take)/gather | solution.py:57
  250.7 13.0 %gather_fusion = bf16[3072,384]{1,0:T(8,128)(2,1)} fusion(bf16[3584,384]{1,0:T(8,128)(2,1)S(1)} %get-tuple-element.187, s32[3072]{0:T(1024)S(1)} %broadcast_clamp_fusion.2), kind=kCustom, calls=%fused_computation.clone.clone.1 | custom fusion | bytes 4730880 | tf_op jit(solution)/shard_map/while/body/eval_jaxpr/jit(_take)/gather | solution.py:57
  271.5 13.0 %gather_fusion = bf16[3072,384]{1,0:T(8,128)(2,1)} fusion(bf16[3584,384]{1,0:T(8,128)(2,1)S(1)} %get-tuple-element.187, s32[3072]{0:T(1024)S(1)} %broadcast_clamp_fusion.2), kind=kCustom, calls=%fused_computation.clone.clone.1 | custom fusion | bytes 4730880 | tf_op jit(solution)/shard_map/while/body/eval_jaxpr/jit(_take)/gather | solution.py:57
  292.2 13.0 %gather_fusion = bf16[3072,384]{1,0:T(8,128)(2,1)} fusion(bf16[3584,384]{1,0:T(8,128)(2,1)S(1)} %get-tuple-element.187, s32[3072]{0:T(1024)S(1)} %broadcast_clamp_fusion.2), kind=kCustom, calls=%fused_computation.clone.clone.1 | custom fusion | bytes 4730880 | tf_op jit(solution)/shard_map/while/body/eval_jaxpr/jit(_take)/gather | solution.py:57
  313.0 13.0 %gather_fusion = bf16[3072,384]{1,0:T(8,128)(2,1)} fusion(bf16[3584,384]{1,0:T(8,128)(2,1)S(1)} %get-tuple-element.187, s32[3072]{0:T(1024)S(1)} %broadcast_clamp_fusion.2), kind=kCustom, calls=%fused_computation.clone.clone.1 | custom fusion | bytes 4730880 | tf_op jit(solution)/shard_map/while/body/eval_jaxpr/jit(_take)/gather | solution.py:57
  354.5 13.0 %gather_fusion = bf16[3072,384]{1,0:T(8,128)(2,1)} fusion(bf16[3584,384]{1,0:T(8,128)(2,1)S(1)} %get-tuple-element.187, s32[3072]{0:T(1024)S(1)} %broadcast_clamp_fusion.2), kind=kCustom, calls=%fused_computation.clone.clone.1 | custom fusion | bytes 4730880 | tf_op jit(solution)/shard_map/while/body/eval_jaxpr/jit(_take)/gather | solution.py:57
  375.2 13.0 %gather_fusion = bf16[3072,384]{1,0:T(8,128)(2,1)} fusion(bf16[3584,384]{1,0:T(8,128)(2,1)S(1)} %get-tuple-element.187, s32[3072]{0:T(1024)S(1)} %broadcast_clamp_fusion.2), kind=kCustom, calls=%fused_computation.clone.clone.1 | custom fusion | bytes 4730880 | tf_op jit(solution)/shard_map/while/body/eval_jaxpr/jit(_take)/gather | solution.py:57
  416.7 13.0 %gather_fusion = bf16[3072,384]{1,0:T(8,128)(2,1)} fusion(bf16[3584,384]{1,0:T(8,128)(2,1)S(1)} %get-tuple-element.187, s32[3072]{0:T(1024)S(1)} %broadcast_clamp_fusion.2), kind=kCustom, calls=%fused_computation.clone.clone.1 | custom fusion | bytes 4730880 | tf_op jit(solution)/shard_map/while/body/eval_jaxpr/jit(_take)/gather | solution.py:57
  437.5 13.0 %gather_fusion = bf16[3072,384]{1,0:T(8,128)(2,1)} fusion(bf16[3584,384]{1,0:T(8,128)(2,1)S(1)} %get-tuple-element.187, s32[3072]{0:T(1024)S(1)} %broadcast_clamp_fusion.2), kind=kCustom, calls=%fused_computation.clone.clone.1 | custom fusion | bytes 4730880 | tf_op jit(solution)/shard_map/while/body/eval_jaxpr/jit(_take)/gather | solution.py:57
  479.0 13.0 %gather_fusion = bf16[3072,384]{1,0:T(8,128)(2,1)} fusion(bf16[3584,384]{1,0:T(8,128)(2,1)S(1)} %get-tuple-element.187, s32[3072]{0:T(1024)S(1)} %broadcast_clamp_fusion.2), kind=kCustom, calls=%fused_computation.clone.clone.1 | custom fusion | bytes 4730880 | tf_op jit(solution)/shard_map/while/body/eval_jaxpr/jit(_take)/gather | solution.py:57
  499.7 13.0 %gather_fusion = bf16[3072,384]{1,0:T(8,128)(2,1)} fusion(bf16[3584,384]{1,0:T(8,128)(2,1)S(1)} %get-tuple-element.187, s32[3072]{0:T(1024)S(1)} %broadcast_clamp_fusion.2), kind=kCustom, calls=%fused_computation.clone.clone.1 | custom fusion | bytes 4730880 | tf_op jit(solution)/shard_map/while/body/eval_jaxpr/jit(_take)/gather | solution.py:57
  541.2 13.0 %gather_fusion = bf16[3072,384]{1,0:T(8,128)(2,1)} fusion(bf16[3584,384]{1,0:T(8,128)(2,1)S(1)} %get-tuple-element.187, s32[3072]{0:T(1024)S(1)} %broadcast_clamp_fusion.2), kind=kCustom, calls=%fused_computation.clone.clone.1 | custom fusion | bytes 4730880 | tf_op jit(solution)/shard_map/while/body/eval_jaxpr/jit(_take)/gather | solution.py:57
  562.0 13.0 %gather_fusion = bf16[3072,384]{1,0:T(8,128)(2,1)} fusion(bf16[3584,384]{1,0:T(8,128)(2,1)S(1)} %get-tuple-element.187, s32[3072]{0:T(1024)S(1)} %broadcast_clamp_fusion.2), kind=kCustom, calls=%fused_computation.clone.clone.1 | custom fusion | bytes 4730880 | tf_op jit(solution)/shard_map/while/body/eval_jaxpr/jit(_take)/gather | solution.py:57
  582.7 13.0 %gather_fusion = bf16[3072,384]{1,0:T(8,128)(2,1)} fusion(bf16[3584,384]{1,0:T(8,128)(2,1)S(1)} %get-tuple-element.187, s32[3072]{0:T(1024)S(1)} %broadcast_clamp_fusion.2), kind=kCustom, calls=%fused_computation.clone.clone.1 | custom fusion | bytes 4730880 | tf_op jit(solution)/shard_map/while/body/eval_jaxpr/jit(_take)/gather | solution.py:57
  664.8 158.6 %all-reduce.7.cloned.1.call-done = f32[27,192,384]{2,1,0:T(8,128)} async-done(((f32[27,192,384]{2,1,0:T(8,128)}), f32[27,192,384]{2,1,0:T(8,128)}) %all-reduce.7.cloned.1.call-update) | async-done | bytes 7962640 | tf_op jit(solution)/shard_map/psum | solution.py:13
  823.5 155.8 %all-reduce.9.cloned.1.call-done = f32[27,192,384]{2,1,0:T(8,128)} async-done(((f32[27,192,384]{2,1,0:T(8,128)}), f32[27,192,384]{2,1,0:T(8,128)}) %all-reduce.9.cloned.1.call-update) | async-done | bytes 7962640 | tf_op jit(solution)/shard_map/psum | solution.py:13
  982.2 153.1 %all-reduce.11.cloned.1.call-done = f32[27,192,384]{2,1,0:T(8,128)} async-done(((f32[27,192,384]{2,1,0:T(8,128)}), f32[27,192,384]{2,1,0:T(8,128)}) %all-reduce.11.cloned.1.call-update) | async-done | bytes 7962640 | tf_op jit(solution)/shard_map/psum | solution.py:13
  (291 shorter events, 395.0 us)
Async XLA Ops:
  7.2 54.2 %copy-start.2 = (bf16[192,3072]{1,0:T(8,128)(2,1)S(1)}, bf16[192,3072]{1,0:T(8,128)(2,1)}, u32[]{:S(2)}) copy-start(bf16[192,3072]{1,0:T(8,128)(2,1)} %param.9) | copy-start | bytes 3538948
  7.2 53.5 %copy-start.4 = (f32[192]{0:T(256)S(1)}, f32[192]{0:T(256)}, u32[]{:S(2)}) copy-start(f32[192]{0:T(256)} %param.10) | copy-start | bytes 2308
  7.2 54.2 %copy-start.3 = (f32[192]{0:T(256)S(1)}, f32[192]{0:T(256)}, u32[]{:S(2)}) copy-start(f32[192]{0:T(256)} %param.11) | copy-start | bytes 2308
  7.2 79.1 %all-gather.2.cloned.1.call-start = ((), (), s32[]{:S(2)}) async-start(), calls=%async_computation | async-start | bytes 3538944 | tf_op jit(solution)/shard_map/all_gather | solution.py:49
  63.1 760.3 %all-reduce.7.cloned.1.call-start = ((), (), s32[]{:S(2)}) async-start(), calls=%async_computation.1 | async-start | bytes 15925248 | tf_op jit(solution)/shard_map/psum | solution.py:13
  87.4 7.2 collective-permute-start
  90.6 7.9 collective-permute-start.1
  139.3 5.1 copy-start
  180.8 5.1 copy-start
  201.5 5.1 copy-start
  243.0 5.1 copy-start
  263.8 5.1 copy-start
  305.3 5.1 copy-start
  326.0 5.1 copy-start
  346.8 5.1 copy-start
  367.5 5.1 copy-start
  388.3 5.1 copy-start
  409.0 5.1 copy-start
  450.5 5.1 copy-start
  471.3 5.1 copy-start
  512.8 5.1 copy-start
  533.5 5.1 copy-start
  664.8 314.5 %all-reduce.9.cloned.1.call-start = ((), (), s32[]{:S(2)}) async-start(), calls=%async_computation.2 | async-start | bytes 15925248 | tf_op jit(solution)/shard_map/psum | solution.py:13
  823.5 311.8 %all-reduce.11.cloned.1.call-start = ((), (), s32[]{:S(2)}) async-start(), calls=%async_computation.3 | async-start | bytes 15925248 | tf_op jit(solution)/shard_map/psum | solution.py:13
  (40 other events, 200.4 us)
Sparse Core Ops, SparseCore 0:
  63.3 23.0 all-gather.1
  664.9 158.5 all-reduce.6
  826.0 153.3 all-reduce.8
  981.7 153.5 all-reduce.10
where the time goes:
time: 1150 us
  waiting for transfers between devices  497 us (43%)
  local copies, waits for them, and re-layouts  366 us (32%)
  matrix products  181 us (16%)
  blocking collectives  48.1 us (4%)
  other arithmetic  36.9 us (3%)
  between operations  14.6 us (1%)
    psum x3, waiting for transfers between devices, region_sum(): x = lax.psum(x, axis)  468 us
    gather x27, local copies, waits for them, and re-layouts, offset_step(): picked = jnp.take(gathered, position, axis=0, mode='fill', fill_value=0)  352 us
    dot_general x27, matrix products, offset_step(): lax.dot_general(kernel, picked, (((1,), (1,)), ((), ())), preferred_eleme...  137 us
    psum x6, blocking collectives, region_sum(): x = lax.psum(x, axis)  48.1 us
    dot_general x27, matrix products, offset_step(): grad_piece = jnp.dot(grad_out, picked, preferred_element_type=jnp.float32)  43.4 us
    select_n x27, other arithmetic, offset_step(): picked = jnp.take(gathered, position, axis=0, mode='fill', fill_value=0)  24.9 us
    all_gather x1, waiting for transfers between devices, per_device(): own_chans = lax.all_gather(site_rows, 'chan', axis=1, tiled=True)  23.1 us
  transfers between devices with their start and end apart: 6, of which 6 were waited for; matrix products, arithmetic and copies ran while one was open for 0% of the time, Pallas kernels for 0%

commit v1 on v0

--- a/solution.py
+++ b/solution.py
@@ -46,7 +46,8 @@
         * live_mask[None, :]
     )
     site_rows = jnp.transpose(normed).astype(jnp.bfloat16)
-    own_chans = lax.all_gather(site_rows, "chan", axis=1, tiled=True)
+    sent = jnp.stack([site_rows] * lax.axis_size("chan"))
+    own_chans = jnp.concatenate(lax.all_to_all(sent, "chan", 0, 0), axis=1)
     gathered = padded(own_chans, border)
     anchor = region_idx * columns - border
     extent = columns + 2 * border

time: 1150 us -> 1140 us (level)
  waiting for transfers between devices: 497 us -> 473 us
  blocking collectives: 48.1 us -> 64.8 us
    all_gather x1 -> x0, waiting for transfers between devices: 23.1 us -> none  [per_device(): own_chans = lax.all_gather(site_rows, 'chan', axis=1, tiled=True)]
    all_to_all x0 -> x1, blocking collectives: none -> 16.7 us  [per_device(): own_chans = jnp.concatenate(lax.all_to_all(sent, 'chan', 0, 0), axis=1)]
  transfers between devices with their start and end apart: 6 -> 5, of which waited for: 6 -> 5; matrix products, arithmetic and copies ran while one was open for 0% -> 0% of each run, Pallas kernels for 0% -> 0%
where the time goes in v1:
time: 1140 us
  waiting for transfers between devices  473 us (41%)
  local copies, waits for them, and re-layouts  365 us (32%)
  matrix products  181 us (16%)
  blocking collectives  64.8 us (6%)
  other arithmetic  34.4 us (3%)
  between operations  14.6 us (1%)
    psum x3, waiting for transfers between devices, region_sum(): x = lax.psum(x, axis)  466 us
    gather x27, local copies, waits for them, and re-layouts, offset_step(): picked = jnp.take(gathered, position, axis=0, mode='fill', fill_value=0)  352 us
    dot_general x27, matrix products, offset_step(): lax.dot_general(kernel, picked, (((1,), (1,)), ((), ())), preferred_eleme...  137 us
    psum x6, blocking collectives, region_sum(): x = lax.psum(x, axis)  48.1 us
    dot_general x27, matrix products, offset_step(): grad_piece = jnp.dot(grad_out, picked, preferred_element_type=jnp.float32)  43.4 us
    select_n x27, other arithmetic, offset_step(): picked = jnp.take(gathered, position, axis=0, mode='fill', fill_value=0)  24.9 us
  transfers between devices with their start and end apart: 5, of which 5 were waited for; matrix products, arithmetic and copies ran while one was open for 0% of the time, Pallas kernels for 0%

profile of v1, /device:TPU:1, one launch (start us, length us, event | category | flops | bytes accessed | tf_op | source)
XLA Modules:
  0.0 1138.2 jit_solution(3007058109829792364)
XLA Ops:
  62.3 16.7 %all_to_all.5 = bf16[2,3072,192]{1,2,0:T(8,128)(2,1)S(1)} all-to-all(bf16[2,3072,192]{1,2,0:T(8,128)(2,1)S(1)} %pad_maximum_fusion.1), channel_id=1, replica_groups=mesh['z'=4,'y'=4,'x'=4,'chan'=2] {'chan'}, dimensions={0} | all-to-all | bytes 4718592 | tf_op jit(solution)/shard_map/all_to_all | solution.py:50
  95.5 559.6 %while.13 = (s32[]{:T(128)}, f32[192,3072]{1,0:T(8,128)}, f32[27,192,384]{2,1,0:T(8,128)}, bf16[27,192,384]{2,1,0:T(8,128)(2,1)}, s32[27,3072]{1,0:T(8,128)}, /*...) while((s32[]{:T(128)}, f32[192,3072]{1,0:T(8,128)}, ...), condition=%wide.region_13.14_spmd.clone, body=%wide.region_12.13_spmd.clone.sunk | while | flops 909548544 | bytes 30030000 | solution.py:66
  116.5 13.0 %gather_fusion = bf16[3072,384]{1,0:T(8,128)(2,1)} fusion(bf16[3584,384]{1,0:T(8,128)(2,1)S(1)} %get-tuple-element.187, s32[3072]{0:T(1024)S(1)} %broadcast_clamp_fusion.2), kind=kCustom, calls=%fused_computation.clone.clone.1 | custom fusion | bytes 4730880 | tf_op jit(solution)/shard_map/while/body/eval_jaxpr/jit(_take)/gather | solution.py:58
  137.3 13.0 %gather_fusion = bf16[3072,384]{1,0:T(8,128)(2,1)} fusion(bf16[3584,384]{1,0:T(8,128)(2,1)S(1)} %get-tuple-element.187, s32[3072]{0:T(1024)S(1)} %broadcast_clamp_fusion.2), kind=kCustom, calls=%fused_computation.clone.clone.1 | custom fusion | bytes 4730880 | tf_op jit(solution)/shard_map/while/body/eval_jaxpr/jit(_take)/gather | solution.py:58
  158.0 13.0 %gather_fusion = bf16[3072,384]{1,0:T(8,128)(2,1)} fusion(bf16[3584,384]{1,0:T(8,128)(2,1)S(1)} %get-tuple-element.187, s32[3072]{0:T(1024)S(1)} %broadcast_clamp_fusion.2), kind=kCustom, calls=%fused_computation.clone.clone.1 | custom fusion | bytes 4730880 | tf_op jit(solution)/shard_map/while/body/eval_jaxpr/jit(_take)/gather | solution.py:58
  178.8 13.0 %gather_fusion = bf16[3072,384]{1,0:T(8,128)(2,1)} fusion(bf16[3584,384]{1,0:T(8,128)(2,1)S(1)} %get-tuple-element.187, s32[3072]{0:T(1024)S(1)} %broadcast_clamp_fusion.2), kind=kCustom, calls=%fused_computation.clone.clone.1 | custom fusion | bytes 4730880 | tf_op jit(solution)/shard_map/while/body/eval_jaxpr/jit(_take)/gather | solution.py:58
  199.5 13.0 %gather_fusion = bf16[3072,384]{1,0:T(8,128)(2,1)} fusion(bf16[3584,384]{1,0:T(8,128)(2,1)S(1)} %get-tuple-element.187, s32[3072]{0:T(1024)S(1)} %broadcast_clamp_fusion.2), kind=kCustom, calls=%fused_computation.clone.clone.1 | custom fusion | bytes 4730880 | tf_op jit(solution)/shard_map/while/body/eval_jaxpr/jit(_take)/gather | solution.py:58
  220.3 13.0 %gather_fusion = bf16[3072,384]{1,0:T(8,128)(2,1)} fusion(bf16[3584,384]{1,0:T(8,128)(2,1)S(1)} %get-tuple-element.187, s32[3072]{0:T(1024)S(1)} %broadcast_clamp_fusion.2), kind=kCustom, calls=%fused_computation.clone.clone.1 | custom fusion | bytes 4730880 | tf_op jit(solution)/shard_map/while/body/eval_jaxpr/jit(_take)/gather | solution.py:58
  241.0 13.0 %gather_fusion = bf16[3072,384]{1,0:T(8,128)(2,1)} fusion(bf16[3584,384]{1,0:T(8,128)(2,1)S(1)} %get-tuple-element.187, s32[3072]{0:T(1024)S(1)} %broadcast_clamp_fusion.2), kind=kCustom, calls=%fused_computation.clone.clone.1 | custom fusion | bytes 4730880 | tf_op jit(solution)/shard_map/while/body/eval_jaxpr/jit(_take)/gather | solution.py:58
  261.8 13.0 %gather_fusion = bf16[3072,384]{1,0:T(8,128)(2,1)} fusion(bf16[3584,384]{1,0:T(8,128)(2,1)S(1)} %get-tuple-element.187, s32[3072]{0:T(1024)S(1)} %broadcast_clamp_fusion.2), kind=kCustom, calls=%fused_computation.clone.clone.1 | custom fusion | bytes 4730880 | tf_op jit(solution)/shard_map/while/body/eval_jaxpr/jit(_take)/gather | solution.py:58
  303.3 13.0 %gather_fusion = bf16[3072,384]{1,0:T(8,128)(2,1)} fusion(bf16[3584,384]{1,0:T(8,128)(2,1)S(1)} %get-tuple-element.187, s32[3072]{0:T(1024)S(1)} %broadcast_clamp_fusion.2), kind=kCustom, calls=%fused_computation.clone.clone.1 | custom fusion | bytes 4730880 | tf_op jit(solution)/shard_map/while/body/eval_jaxpr/jit(_take)/gather | solution.py:58
  324.0 13.0 %gather_fusion = bf16[3072,384]{1,0:T(8,128)(2,1)} fusion(bf16[3584,384]{1,0:T(8,128)(2,1)S(1)} %get-tuple-element.187, s32[3072]{0:T(1024)S(1)} %broadcast_clamp_fusion.2), kind=kCustom, calls=%fused_computation.clone.clone.1 | custom fusion | bytes 4730880 | tf_op jit(solution)/shard_map/while/body/eval_jaxpr/jit(_take)/gather | solution.py:58
  365.5 13.0 %gather_fusion = bf16[3072,384]{1,0:T(8,128)(2,1)} fusion(bf16[3584,384]{1,0:T(8,128)(2,1)S(1)} %get-tuple-element.187, s32[3072]{0:T(1024)S(1)} %broadcast_clamp_fusion.2), kind=kCustom, calls=%fused_computation.clone.clone.1 | custom fusion | bytes 4730880 | tf_op jit(solution)/shard_map/while/body/eval_jaxpr/jit(_take)/gather | solution.py:58
  386.3 13.0 %gather_fusion = bf16[3072,384]{1,0:T(8,128)(2,1)} fusion(bf16[3584,384]{1,0:T(8,128)(2,1)S(1)} %get-tuple-element.187, s32[3072]{0:T(1024)S(1)} %broadcast_clamp_fusion.2), kind=kCustom, calls=%fused_computation.clone.clone.1 | custom fusion | bytes 4730880 | tf_op jit(solution)/shard_map/while/body/eval_jaxpr/jit(_take)/gather | solution.py:58
  427.8 13.0 %gather_fusion = bf16[3072,384]{1,0:T(8,128)(2,1)} fusion(bf16[3584,384]{1,0:T(8,128)(2,1)S(1)} %get-tuple-element.187, s32[3072]{0:T(1024)S(1)} %broadcast_clamp_fusion.2), kind=kCustom, calls=%fused_computation.clone.clone.1 | custom fusion | bytes 4730880 | tf_op jit(solution)/shard_map/while/body/eval_jaxpr/jit(_take)/gather | solution.py:58
  448.5 13.0 %gather_fusion = bf16[3072,384]{1,0:T(8,128)(2,1)} fusion(bf16[3584,384]{1,0:T(8,128)(2,1)S(1)} %get-tuple-element.187, s32[3072]{0:T(1024)S(1)} %broadcast_clamp_fusion.2), kind=kCustom, calls=%fused_computation.clone.clone.1 | custom fusion | bytes 4730880 | tf_op jit(solution)/shard_map/while/body/eval_jaxpr/jit(_take)/gather | solution.py:58
  490.0 13.0 %gather_fusion = bf16[3072,384]{1,0:T(8,128)(2,1)} fusion(bf16[3584,384]{1,0:T(8,128)(2,1)S(1)} %get-tuple-element.187, s32[3072]{0:T(1024)S(1)} %broadcast_clamp_fusion.2), kind=kCustom, calls=%fused_computation.clone.clone.1 | custom fusion | bytes 4730880 | tf_op jit(solution)/shard_map/while/body/eval_jaxpr/jit(_take)/gather | solution.py:58
  510.8 13.0 %gather_fusion = bf16[3072,384]{1,0:T(8,128)(2,1)} fusion(bf16[3584,384]{1,0:T(8,128)(2,1)S(1)} %get-tuple-element.187, s32[3072]{0:T(1024)S(1)} %broadcast_clamp_fusion.2), kind=kCustom, calls=%fused_computation.clone.clone.1 | custom fusion | bytes 4730880 | tf_op jit(solution)/shard_map/while/body/eval_jaxpr/jit(_take)/gather | solution.py:58
  531.5 13.0 %gather_fusion = bf16[3072,384]{1,0:T(8,128)(2,1)} fusion(bf16[3584,384]{1,0:T(8,128)(2,1)S(1)} %get-tuple-element.187, s32[3072]{0:T(1024)S(1)} %broadcast_clamp_fusion.2), kind=kCustom, calls=%fused_computation.clone.clone.1 | custom fusion | bytes 4730880 | tf_op jit(solution)/shard_map/while/body/eval_jaxpr/jit(_take)/gather | solution.py:58
  552.3 13.0 %gather_fusion = bf16[3072,384]{1,0:T(8,128)(2,1)} fusion(bf16[3584,384]{1,0:T(8,128)(2,1)S(1)} %get-tuple-element.187, s32[3072]{0:T(1024)S(1)} %broadcast_clamp_fusion.2), kind=kCustom, calls=%fused_computation.clone.clone.1 | custom fusion | bytes 4730880 | tf_op jit(solution)/shard_map/while/body/eval_jaxpr/jit(_take)/gather | solution.py:58
  573.0 13.0 %gather_fusion = bf16[3072,384]{1,0:T(8,128)(2,1)} fusion(bf16[3584,384]{1,0:T(8,128)(2,1)S(1)} %get-tuple-element.187, s32[3072]{0:T(1024)S(1)} %broadcast_clamp_fusion.2), kind=kCustom, calls=%fused_computation.clone.clone.1 | custom fusion | bytes 4730880 | tf_op jit(solution)/shard_map/while/body/eval_jaxpr/jit(_take)/gather | solution.py:58
  655.1 157.3 %all-reduce.7.cloned.1.call-done = f32[27,192,384]{2,1,0:T(8,128)} async-done(((f32[27,192,384]{2,1,0:T(8,128)}), f32[27,192,384]{2,1,0:T(8,128)}) %all-reduce.7.cloned.1.call-update) | async-done | bytes 7962640 | tf_op jit(solution)/shard_map/psum | solution.py:13
  812.5 155.8 %all-reduce.9.cloned.1.call-done = f32[27,192,384]{2,1,0:T(8,128)} async-done(((f32[27,192,384]{2,1,0:T(8,128)}), f32[27,192,384]{2,1,0:T(8,128)}) %all-reduce.9.cloned.1.call-update) | async-done | bytes 7962640 | tf_op jit(solution)/shard_map/psum | solution.py:13
  971.1 153.2 %all-reduce.11.cloned.1.call-done = f32[27,192,384]{2,1,0:T(8,128)} async-done(((f32[27,192,384]{2,1,0:T(8,128)}), f32[27,192,384]{2,1,0:T(8,128)}) %all-reduce.11.cloned.1.call-update) | async-done | bytes 7962640 | tf_op jit(solution)/shard_map/psum | solution.py:13
  (290 shorter events, 391.7 us)
Async XLA Ops:
  7.2 54.2 %copy-start.2 = (bf16[192,3072]{1,0:T(8,128)(2,1)S(1)}, bf16[192,3072]{1,0:T(8,128)(2,1)}, u32[]{:S(2)}) copy-start(bf16[192,3072]{1,0:T(8,128)(2,1)} %param.9) | copy-start | bytes 3538948
  7.2 53.5 %copy-start.4 = (f32[192]{0:T(256)S(1)}, f32[192]{0:T(256)}, u32[]{:S(2)}) copy-start(f32[192]{0:T(256)} %param.10) | copy-start | bytes 2308
  7.2 54.2 %copy-start.3 = (f32[192]{0:T(256)S(1)}, f32[192]{0:T(256)}, u32[]{:S(2)}) copy-start(f32[192]{0:T(256)} %param.11) | copy-start | bytes 2308
  7.2 805.2 %all-reduce.7.cloned.1.call-start = ((), (), s32[]{:S(2)}) async-start(), calls=%async_computation.1 | async-start | bytes 15925248 | tf_op jit(solution)/shard_map/psum | solution.py:13
  79.1 7.5 collective-permute-start
  82.7 7.7 collective-permute-start.1
  129.6 5.1 copy-start
  150.3 5.1 copy-start
  191.8 5.1 copy-start
  212.6 5.1 copy-start
  254.1 5.1 copy-start
  274.8 5.1 copy-start
  295.6 5.1 copy-start
  316.3 5.1 copy-start
  337.1 5.1 copy-start
  357.8 5.1 copy-start
  399.3 5.1 copy-start
  420.1 5.1 copy-start
  461.6 5.1 copy-start
  482.3 5.1 copy-start
  523.8 5.1 copy-start
  544.6 5.1 copy-start
  655.1 313.2 %all-reduce.9.cloned.1.call-start = ((), (), s32[]{:S(2)}) async-start(), calls=%async_computation.2 | async-start | bytes 15925248 | tf_op jit(solution)/shard_map/psum | solution.py:13
  812.5 311.9 %all-reduce.11.cloned.1.call-start = ((), (), s32[]{:S(2)}) async-start(), calls=%async_computation.3 | async-start | bytes 15925248 | tf_op jit(solution)/shard_map/psum | solution.py:13
  (39 other events, 195.3 us)
Sparse Core Ops, SparseCore 0:
  655.2 157.1 all-reduce.6
  814.9 153.3 all-reduce.8
  970.8 153.5 all-reduce.10
